TPU v7x, 256 devices: a whole 4x4x8 slice. The times are simulated.
256 devices in a mesh: grp: 32 (over z, x), tp: 8 (over y, core).
Axes of the slice: x: 4, y: 4, z: 8, core: 2. Of those that a mesh axis runs over, the one named last changes fastest.
Arguments:
- tokens: bfloat16 [32768, 2048], P('grp'), may hold values from -6 to 6
- norm_gain: float32 [2048], replicated, may hold values from 0.5 to 7
- w_qkv: bfloat16 [2048, 3, 2048], P(None, None, 'tp'), may hold values from -0.125 to 0.125
- w_out: bfloat16 [2048, 2048], P('tp'), may hold values from -0.125 to 0.125
- a_in: bfloat16 [64, 2048, 48], P('grp', 'tp'), may hold values from -0.125 to 0.125
- b_in: bfloat16 [64, 3, 16, 2048], P('grp', None, None, 'tp'), may hold values from -1.5 to 1.5
- a_out: bfloat16 [64, 2048, 16], P('grp', 'tp'), may hold values from -0.125 to 0.125
- b_out: bfloat16 [64, 16, 2048], P('grp', None, 'tp'), may hold values from -1.5 to 1.5
- req_len: int32 [32, 4], replicated, may hold values from 1 to 512, 1024 in all within a row
- req_adapter: int32 [32, 4], replicated, may hold values from 0 to 63, as said below
- holder: int32 [64], replicated, may hold values from 0 to 63, each once
- page_table: int32 [32, 8], P('grp'), may hold values from 0 to 7, each once within a row
Outputs:
- layer_out: bfloat16 [32768, 2048], P('grp', 'tp')
- kv_pages: bfloat16 [256, 2, 128, 2048], P('grp', None, None, 'tp')
Inputs may be any that keep to these rules, and one draw needn't show every extreme that they name: `req_adapter`: exactly 16 different adapters appear among all requests.
All inputs are finite; a program needn't handle non-finite values.
Results may differ from a plain program's by a relative error of at most 0.017.
The roundings to bfloat16 on the way count: a program that leaves them out, or rounds other values in their place, can miss the bound.
Values may be sent and summed in bfloat16 or wider, within the bound.
No kernel may reach another device: no remote copies, remote signals or barrier semaphores. Data moves between devices by JAX's collectives and lax.ppermute only.
A program may use at most 128 MiB of HBM per device.

v0:
```python
import math
import jax
import jax.numpy as jnp
from jax import lax
from jax.sharding import PartitionSpec as P

HD = 128
PAGE = 128
EPSILON = 1e-05
THETA = 10000.0


def shifted(block, axis, distance):
    devices = range(lax.axis_size(axis))
    route = [(i - distance, i) for i in devices if i - distance in devices]
    return lax.ppermute(block, axis, route)


USED = 16


def xor_allreduce(value, axis):
    count = lax.axis_size(axis)
    step = 1
    while step < count:
        route = [(i, i ^ step) for i in range(count)]
        value = value + lax.ppermute(value, axis, route)
        step *= 2
    return value


def fetch_adapters(stores, req_adapter, holder, wanted, group_id):
    held = stores[0].shape[0]
    total = holder.shape[0]
    names = jnp.arange(total, dtype=jnp.int32)
    used = jnp.any(req_adapter.reshape(-1)[:, None] == names[None, :], axis=0)
    rank = jnp.cumsum(used.astype(jnp.int32)) - 1
    picks = jnp.arange(USED, dtype=jnp.int32)
    hit = used[None, :] & (rank[None, :] == picks[:, None])
    chosen = jnp.sum(jnp.where(hit, names[None, :], 0), axis=1)
    slots = holder[chosen]
    mine = slots // held == group_id
    local_idx = slots % held
    flat = jnp.concatenate([s.reshape(held, -1) for s in stores], axis=1)
    compact = jnp.where(mine[:, None], jnp.take(flat, local_idx, axis=0), jnp.zeros((), flat.dtype))
    compact = lax.psum(compact, "grp")
    mine_rows = jnp.take(compact, rank[wanted], axis=0)
    out = []
    at = 0
    for s in stores:
        size = math.prod(s.shape[1:])
        out.append(mine_rows[:, at : at + size].reshape((wanted.shape[0],) + s.shape[1:]))
        at += size
    return tuple(out)


def rms_norm(token_rows, norm_gain):
    values = token_rows.astype(jnp.float32)
    norm_scale = lax.rsqrt(jnp.mean(values * values, axis=-1, keepdims=True) + EPSILON)
    return (values * norm_scale * norm_gain).astype(jnp.bfloat16)


def request_layout(lengths, offset, tok_count):
    end_at = jnp.cumsum(lengths)
    starts = end_at - lengths
    row_ids = jnp.arange(tok_count, dtype=jnp.int32)
    segment = jnp.sum((row_ids[:, None] >= end_at[None, :]).astype(jnp.int32), axis=1)
    member = segment[:, None] == jnp.arange(lengths.shape[0], dtype=jnp.int32)[None, :]
    begin_at = jnp.sum(jnp.where(member, starts[None, :], 0), axis=1)
    position = row_ids - begin_at + jnp.where(segment == 0, offset, 0)
    return (segment, member, position)


def rotate(head_rows, position, head_dim):
    half_dim = head_dim // 2
    frequency = THETA ** (-(jnp.arange(half_dim, dtype=jnp.float32) * (2.0 / head_dim)))
    angles = position.astype(jnp.float32)[:, None] * frequency[None, :]
    cosine = jnp.cos(angles)[:, None, :]
    sine_part = jnp.sin(angles)[:, None, :]
    lower_half = head_rows[..., :half_dim]
    upper_half = head_rows[..., half_dim:]
    return jnp.concatenate(
        [
            lower_half * cosine - upper_half * sine_part,
            upper_half * cosine + lower_half * sine_part,
        ],
        axis=-1,
    )


def local(
    tokens,
    norm_gain,
    w_qkv,
    w_out,
    a_in,
    b_in,
    a_out,
    b_out,
    req_len,
    req_adapter,
    holder,
    page_table,
):
    tok_count = tokens.shape[0]
    local_width = w_out.shape[0]
    local_heads = local_width // HD
    req_count = req_len.shape[1]
    rank_dim = a_out.shape[2]
    group_id = lax.axis_index("grp")
    tp_id = lax.axis_index("tp")
    lengths = lax.dynamic_index_in_dim(req_len, group_id, 0, keepdims=False)
    earlier = lax.dynamic_index_in_dim(req_len, jnp.maximum(group_id - 1, 0), 0, keepdims=False)
    continued = group_id > 0
    prev_len = earlier[req_count - 1]
    offset = jnp.where(continued, prev_len, 0)
    segment, member, position = request_layout(lengths, offset, tok_count)
    wanted = lax.dynamic_index_in_dim(req_adapter, group_id, 0, keepdims=False)
    sel_in, sel_up, sel_odown, sel_oup = fetch_adapters(
        (a_in, b_in, a_out, b_out), req_adapter, holder, wanted, group_id
    )
    member_f = member.astype(jnp.float32)
    pick_bf = member.astype(jnp.bfloat16)
    normed = rms_norm(tokens, norm_gain)
    own_cols = lax.dynamic_slice_in_dim(normed, tp_id * local_width, local_width, 1)
    down_f = jnp.einsum("td,rdk->trk", own_cols, sel_in, preferred_element_type=jnp.float32)
    lowrank_f = xor_allreduce(jnp.sum(down_f * member_f[:, :, None], axis=1), "tp")
    lowrank = lowrank_f.astype(jnp.bfloat16)
    spread = (pick_bf[:, :, None] * lowrank[:, None, :]).reshape(tok_count, req_count, 3, rank_dim)
    delta_qkv = jnp.einsum("trck,rckd->tcd", spread, sel_up, preferred_element_type=jnp.float32)
    base_qkv = jnp.dot(
        normed, w_qkv.reshape(w_qkv.shape[0], 3 * local_width), preferred_element_type=jnp.float32
    )
    qkv = (base_qkv.reshape(tok_count, 3, local_width) + delta_qkv).reshape(
        tok_count, 3, local_heads, HD
    )
    query_rows = rotate(qkv[:, 0], position, HD).astype(jnp.bfloat16)
    key_rows = rotate(qkv[:, 1], position, HD).astype(jnp.bfloat16).reshape(tok_count, local_width)
    value_rows = qkv[:, 2].astype(jnp.bfloat16).reshape(tok_count, local_width)
    row_ids = jnp.arange(tok_count, dtype=jnp.int32)
    far_key, far_value = shifted((key_rows, value_rows), "grp", 1)
    far_ok = continued & (segment[:, None] == 0) & (row_ids[None, :] >= tok_count - prev_len)
    far_count = far_key.shape[0]
    near_ok = (segment[:, None] == segment[None, :]) & (row_ids[None, :] <= row_ids[:, None])
    allowed = jnp.concatenate([far_ok, near_ok], axis=1)
    key_all = jnp.concatenate([far_key, key_rows], axis=0).reshape(
        far_count + tok_count, local_heads, HD
    )
    value_all = jnp.concatenate([far_value, value_rows], axis=0).reshape(
        far_count + tok_count, local_heads, HD
    )
    score_scale = 1.0 / math.sqrt(HD)
    scores = (
        jnp.einsum("thd,shd->hts", query_rows, key_all, preferred_element_type=jnp.float32)
        * score_scale
    )
    scores = jnp.where(allowed[None], scores, -jnp.inf)
    row_top = jnp.max(scores, axis=-1, keepdims=True)
    weights = jnp.exp(scores - row_top)
    weights_bf = (weights / jnp.sum(weights, axis=-1, keepdims=True)).astype(jnp.bfloat16)
    mixed_heads = jnp.einsum(
        "hts,shd->thd", weights_bf, value_all, preferred_element_type=jnp.float32
    )
    attended = mixed_heads.astype(jnp.bfloat16).reshape(tok_count, local_width)
    partial_value = jnp.dot(attended, w_out, preferred_element_type=jnp.float32)
    down_o = jnp.einsum("td,rdk->trk", attended, sel_odown, preferred_element_type=jnp.float32)
    low_part = jnp.sum(down_o * member_f[:, :, None], axis=1).astype(jnp.bfloat16)
    n_tp = lax.axis_size("tp")
    packed = jnp.concatenate(
        [
            partial_value.astype(jnp.bfloat16).reshape(tok_count, n_tp, local_width),
            jnp.broadcast_to(low_part[:, None, :], (tok_count, n_tp, rank_dim)),
        ],
        axis=2,
    ).reshape(tok_count, n_tp * (local_width + rank_dim))
    summed = lax.psum_scatter(packed, "tp", scatter_dimension=1, tiled=True)
    base_out = summed[:, :local_width].astype(jnp.float32)
    low_o = summed[:, local_width:]
    spread_o = (pick_bf[:, :, None] * low_o[:, None, :]).reshape(tok_count, req_count * rank_dim)
    delta_o = jnp.dot(
        spread_o,
        sel_oup.reshape(req_count * rank_dim, local_width),
        preferred_element_type=jnp.float32,
    )
    own_rows = lax.dynamic_slice_in_dim(tokens, tp_id * local_width, local_width, 1).astype(
        jnp.float32
    )
    layer_out = (own_rows + base_out + delta_o).astype(jnp.bfloat16)
    page_row = page_table[0]
    page_count = page_row.shape[0]
    numbers = jnp.arange(page_count, dtype=jnp.int32)
    inverse = jnp.sum(jnp.where(page_row[:, None] == numbers[None, :], numbers[:, None], 0), axis=0)
    both_blocks = jnp.stack(
        [
            key_rows.reshape(page_count, PAGE, local_width),
            value_rows.reshape(page_count, PAGE, local_width),
        ],
        axis=1,
    )
    kv_pages = jnp.take(both_blocks, inverse, axis=0)
    return (layer_out, kv_pages)


def solution(mesh):
    return jax.shard_map(
        local,
        mesh=mesh,
        in_specs=(
            P("grp", None),
            P(),
            P(None, None, "tp"),
            P("tp", None),
            P("grp", "tp", None),
            P("grp", None, None, "tp"),
            P("grp", "tp", None),
            P("grp", None, "tp"),
            P(),
            P(),
            P(),
            P("grp", None),
        ),
        out_specs=(P("grp", "tp"), P("grp", None, None, "tp")),
        check_vma=False,
    )
```

profile of v0, /device:TPU:4, one launch (start us, length us, event | category | flops | bytes accessed | tf_op | source)
XLA Modules:
  0.0 312.4 jit_solution(5977130857267515130)
XLA Ops:
  19.6 3.1 fusion.2
  23.4 4.7 %copy.62 = bf16[2048,3,256]{0,2,1:T(8,128)(2,1)} copy(bf16[2048,3,256]{2,0,1:T(8,128)(2,1)} %param.14) | data formatting | bytes 6291456 | tf_op args[2]
  28.6 3.5 %fusion.4 = bf16[1024,2048]{1,0:T(8,128)(2,1)S(1)} fusion(bf16[1024,2048]{1,0:T(8,128)(2,1)} %param.12, f32[2048]{0:T(1024)S(1)} %copy-done.7, f32[1024]{0:T(1024)S(1)} %add_rsqrt_fusion), kind=kLoop, calls=%fused_computation.14 | loop fusion | flops 8388608 | bytes 8400896 | tf_op jit(solution)/shard_map/convert_element_type | solution.py:60
  32.2 1.9 copy-done.2
  34.1 5.1 %fusion.9 = f32[1024,3,256]{0,2,1:T(8,128)} fusion(bf16[1024,2048]{1,0:T(8,128)(2,1)S(1)} %fusion.4, bf16[2048,3,256]{0,2,1:T(8,128)(2,1)S(1)} %copy-done.3), kind=kOutput, calls=%fused_computation.21 | convolution fusion | flops 3221225472 | bytes 10485760 | tf_op jit(solution)/shard_map/dot_general | solution.py:131
  39.2 129.0 %all-reduce.2.cloned.1.call-done = bf16[16,32768]{1,0:T(8,128)(2,1)} async-done(((bf16[16,32768]{1,0:T(8,128)(2,1)}), bf16[16,32768]{1,0:T(8,128)(2,1)}) %all-reduce.2.cloned.1.call-update) | async-done | bytes 1048592 | tf_op jit(solution)/shard_map/psum | solution.py:46
  168.2 2.4 gather_fusion.3
  177.3 3.0 multiply_cosine_fusion
  180.3 2.8 collective-permute-done.1
  183.1 3.3 %collective-permute-start.2 = (f32[1024,48]{0,1:T(8,128)S(1)}, f32[1024,48]{0,1:T(8,128)S(1)}, u32[]{:S(2)}, u32[]{:S(2)}) collective-permute-start(f32[1024,48]{0,1:T(8,128)S(1)} %add.163), channel_id=1, source_target_pairs={{0,4},{1,5},{2,6},{3,7},{4,0},{5,1},{6,2},{7,3},{8,12},{9,13},{10,... | collective-permute-start | bytes 589832 | tf_op jit(solution)/shard_map/ppermute | solution.py:27
  187.6 3.7 %collective-permute-done.2 = f32[1024,48]{0,1:T(8,128)S(1)} collective-permute-done((f32[1024,48]{0,1:T(8,128)S(1)}, f32[1024,48]{0,1:T(8,128)S(1)}, u32[]{:S(2)}, u32[]{:S(2)}) %collective-permute-start.2) | collective-permute-done | bytes 196640 | tf_op jit(solution)/shard_map/ppermute | solution.py:27
  191.3 2.5 bitcast_add_fusion
  197.1 3.2 %collective-permute-start.3 = (bf16[1024,256]{0,1:T(8,128)(2,1)}, bf16[1024,256]{0,1:T(8,128)(2,1)}, u32[]{:S(2)}, u32[]{:S(2)}) collective-permute-start(bf16[1024,256]{0,1:T(8,128)(2,1)} %bitcast.106), channel_id=1, source_target_pairs={{0,8},{8,16},{16,24},{24,32},{32,40},{40,48},{48,56},{56,64},{64,7... | collective-permute-start | bytes 1572872 | tf_op jit(solution)/shard_map/ppermute | solution.py:16
  201.9 1.6 multiply_subtract_fusion
  204.8 4.1 %collective-permute-start.4 = (bf16[1024,256]{0,1:T(8,128)(2,1)}, bf16[1024,256]{0,1:T(8,128)(2,1)}, u32[]{:S(2)}, u32[]{:S(2)}) collective-permute-start(bf16[1024,256]{0,1:T(8,128)(2,1)} %bitcast.29), channel_id=1, source_target_pairs={{0,8},{8,16},{16,24},{24,32},{32,40},{40,48},{48,56},{56,64},{64,7... | collective-permute-start | bytes 1572872 | tf_op jit(solution)/shard_map/ppermute | solution.py:16
  210.3 2.6 subtract_convert_fusion
  212.9 10.3 %collective-permute-done.4 = bf16[1024,256]{0,1:T(8,128)(2,1)} collective-permute-done((bf16[1024,256]{0,1:T(8,128)(2,1)}, bf16[1024,256]{0,1:T(8,128)(2,1)}, u32[]{:S(2)}, u32[]{:S(2)}) %collective-permute-start.4) | collective-permute-done | bytes 524320 | tf_op jit(solution)/shard_map/ppermute | solution.py:16
  224.5 10.8 %fusion.49 = (f32[2,1024]{1,0:T(2,128)S(1)}, f32[2,1024,2048]{2,1,0:T(8,128)}) fusion(pred[1024,2048]{1,0:T(8,128)(4,1)} %pad_add_fusion, bf16[1024,2,128]{2,0,1:T(8,128)(2,1)S(1)} %maximum_convert_fusion, bf16[1024,2,128]{2,0,1:T(8,128)(2,1)S(1)} %copy.72, bf16[1024,2,64]{2,0,1:T(8,128)(2,1)} %get-tuple-element.7, bf16[1024,2,64]{2,0,1:T(8,128)(2,1)} %get-tuple-element.6), kind=kOutput, calls=%fused_computation.127 | convolution fusion | flops 1093666816 | bytes 20455424 | tf_op jit(solution)/shard_map/sub | solution.py:159
  235.3 8.9 %fusion.16 = bf16[2,128,1024]{2,1,0:T(8,128)(2,1)S(1)} fusion(f32[2,1024,2048]{2,1,0:T(8,128)} %get-tuple-element.23, f32[2,1024]{1,0:T(2,128)S(1)} %get-tuple-element.22, bf16[1024,2,128]{0,2,1:T(8,128)(2,1)S(1)} %slice_bitcast_fusion, bf16[1024,2,128]{0,2,1:T(8,128)(2,1)} %bitcast.22), kind=kOutput, calls=%fused_computation.32 | convolution fusion | flops 1084489728 | bytes 18358272 | tf_op jit(solution)/shard_map/hts,shd->thd/dot_general | solution.py:161
  244.5 3.2 %convolution_convert_fusion = bf16[1024,2048]{1,0:T(8,128)(2,1)} fusion(bf16[1024,256]{0,1:T(8,128)(2,1)S(1)} %bitcast.104, bf16[256,2048]{1,0:T(8,128)(2,1)S(1)} %copy-done), kind=kOutput, calls=%fused_computation.25 | convolution fusion | flops 1075838976 | bytes 5767168 | tf_op jit(solution)/shard_map/dot_general | solution.py:165
  247.7 6.4 %copy.82 = bf16[1024,2048]{0,1:T(8,128)(2,1)} copy(bf16[1024,2048]{1,0:T(8,128)(2,1)} %convolution_convert_fusion) | data formatting | bytes 8388608 | tf_op jit(solution)/shard_map/reshape | solution.py:171
  254.1 4.7 %pad_maximum_fusion = bf16[1024,8,272]{0,2,1:T(8,128)(2,1)} fusion(bf16[1024,8,16]{0,2,1:T(8,128)(2,1)S(1)} %broadcast_in_dim.158, bf16[1024,8,256]{0,2,1:T(8,128)(2,1)} %bitcast.97), kind=kLoop, calls=%fused_computation.20 | loop fusion | flops 8912896 | bytes 8912896 | tf_op jit(solution)/shard_map/concatenate | solution.py:169
  264.7 36.7 %reduce-scatter.4.cloned.1.call-done = bf16[272,1024]{1,0:T(8,128)(2,1)} async-done(((bf16[2176,1024]{1,0:T(8,128)(2,1)}), bf16[272,1024]{1,0:T(8,128)(2,1)}) %reduce-scatter.4.cloned.1.call-update) | async-done | bytes 557072
  303.4 2.2 fusion.15
  (114 shorter events, 36.8 us)
Async XLA Ops:
  7.2 237.3 %copy-start = (bf16[256,2048]{1,0:T(8,128)(2,1)S(1)}, bf16[256,2048]{1,0:T(8,128)(2,1)}, u32[]{:S(2)}) copy-start(bf16[256,2048]{1,0:T(8,128)(2,1)} %param.15) | copy-start | bytes 3145732
  7.2 161.0 %all-reduce.2.cloned.1.call-start = ((), (), s32[]{:S(2)}) async-start(), calls=%async_computation.1 | async-start | bytes 2097152 | tf_op jit(solution)/shard_map/psum | solution.py:46
  14.0 2.5 copy-start.8
  14.0 2.5 copy-start.9
  16.4 284.9 %reduce-scatter.4.cloned.1.call-start = ((), (), s32[]{:S(2)}) async-start(), calls=%async_computation.2 | async-start | bytes 5013504
  22.7 5.9 %copy-start.7 = (f32[2048]{0:T(1024)S(1)}, f32[2048]{0:T(1024)}, u32[]{:S(2)}) copy-start(f32[2048]{0:T(1024)} %param.13) | copy-start | bytes 24580
  28.6 5.4 %copy-start.3 = (bf16[2048,3,256]{0,2,1:T(8,128)(2,1)S(1)}, bf16[2048,3,256]{0,2,1:T(8,128)(2,1)}, u32[]{:S(2)}) copy-start(bf16[2048,3,256]{0,2,1:T(8,128)(2,1)} %copy.62) | copy-start | bytes 9437188
  32.1 1.9 copy-start.2
  170.8 0.7 copy-start.5
  172.6 14.6 %copy-start.6 = (bf16[4,12288]{1,0:T(4,128)(2,1)S(1)}, bf16[4,12288]{1,0:T(4,128)(2,1)}, u32[]{:S(2)}) copy-start(bf16[4,12288]{1,0:T(4,128)(2,1)} %get-tuple-element.13) | copy-start | bytes 294916
  174.1 1.6 collective-permute-start
  175.7 7.4 %collective-permute-start.1 = (f32[1024,48]{0,1:T(8,128)S(1)}, f32[1024,48]{0,1:T(8,128)S(1)}, u32[]{:S(2)}, u32[]{:S(2)}) collective-permute-start(f32[1024,48]{0,1:T(8,128)S(1)} %add.162), channel_id=1, source_target_pairs={{0,2},{1,3},{2,0},{3,1},{4,6},{5,7},{6,4},{7,5},{8,10},{9,11},{10,... | collective-permute-start | bytes 589832 | tf_op jit(solution)/shard_map/ppermute | solution.py:27
  183.1 8.2 %collective-permute-start.2 = (f32[1024,48]{0,1:T(8,128)S(1)}, f32[1024,48]{0,1:T(8,128)S(1)}, u32[]{:S(2)}, u32[]{:S(2)}) collective-permute-start(f32[1024,48]{0,1:T(8,128)S(1)} %add.163), channel_id=1, source_target_pairs={{0,4},{1,5},{2,6},{3,7},{4,0},{5,1},{6,2},{7,3},{8,12},{9,13},{10,... | collective-permute-start | bytes 589832 | tf_op jit(solution)/shard_map/ppermute | solution.py:27
  193.8 1.8 copy-start.1
  197.1 38.1 %collective-permute-start.3 = (bf16[1024,256]{0,1:T(8,128)(2,1)}, bf16[1024,256]{0,1:T(8,128)(2,1)}, u32[]{:S(2)}, u32[]{:S(2)}) collective-permute-start(bf16[1024,256]{0,1:T(8,128)(2,1)} %bitcast.106), channel_id=1, source_target_pairs={{0,8},{8,16},{16,24},{24,32},{32,40},{40,48},{48,56},{56,64},{64,7... | collective-permute-start | bytes 1572872 | tf_op jit(solution)/shard_map/ppermute | solution.py:16
  204.8 18.3 %collective-permute-start.4 = (bf16[1024,256]{0,1:T(8,128)(2,1)}, bf16[1024,256]{0,1:T(8,128)(2,1)}, u32[]{:S(2)}, u32[]{:S(2)}) collective-permute-start(bf16[1024,256]{0,1:T(8,128)(2,1)} %bitcast.29), channel_id=1, source_target_pairs={{0,8},{8,16},{16,24},{24,32},{32,40},{40,48},{48,56},{56,64},{64,7... | collective-permute-start | bytes 1572872 | tf_op jit(solution)/shard_map/ppermute | solution.py:16
  258.8 0.7 copy-start.10
  258.8 1.3 copy-start.4
Sparse Core Ops, SparseCore 0:
  16.6 151.6 all-reduce.1
  259.0 42.3 reduce-scatter.3
where the time goes:
time: 314 us; the launch traced here: 312 us
  waiting for transfers between devices  183 us (58%)
  local copies, waits for them, and re-layouts  40.9 us (13%)
  matrix products  34.3 us (11%)
  other arithmetic  26.4 us (8%)
  between operations  15.9 us (5%)
  starting transfers between devices  12.3 us (4%)
    psum x1, waiting for transfers between devices, fetch_adapters(): compact = lax.psum(compact, 'grp')  129 us
    unnamed x3, waiting for transfers between devices  36.7 us
    unnamed x34, local copies, waits for them, and re-layouts  15.3 us
    sub x1, matrix products, local(): weights = jnp.exp(scores - row_top)  10.8 us
    ppermute x2, waiting for transfers between devices, shifted(): return lax.ppermute(block, axis, route)  10.3 us
    dot_general x1, matrix products, local(): jnp.einsum('hts,shd->thd', weights_bf, value_all, preferred_element_type=...  8.93 us
    ppermute x2, starting transfers between devices, shifted(): return lax.ppermute(block, axis, route)  7.3 us
    ppermute x3, waiting for transfers between devices, xor_allreduce(): value = value + lax.ppermute(value, axis, route)  6.53 us
  transfers between devices with their start and end apart: 7, of which 5 were waited for; matrix products, arithmetic and copies ran while one was open for 16% of the time, Pallas kernels for 0%

commit v1 on v0

--- a/solution.py
+++ b/solution.py
@@ -43,7 +43,9 @@
     local_idx = slots % held
     flat = jnp.concatenate([s.reshape(held, -1) for s in stores], axis=1)
     compact = jnp.where(mine[:, None], jnp.take(flat, local_idx, axis=0), jnp.zeros((), flat.dtype))
-    compact = lax.psum(compact, "grp")
+    compact = compact
+    for hop in (1, 2, 4, 8, 16):
+        compact = compact + lax.ppermute(compact, "grp", [(dev, dev ^ hop) for dev in range(32)])
     mine_rows = jnp.take(compact, rank[wanted], axis=0)
     out = []
     at = 0

time: 314 us -> 334 us (1.064)
  starting transfers between devices: 12.3 us -> 23.8 us
  waiting for transfers between devices: 183 us -> 192 us
  other arithmetic: 26.4 us -> 29.9 us
  local copies, waits for them, and re-layouts: 40.9 us -> 37.5 us
    ppermute x0 -> x5, waiting for transfers between devices: none -> 138 us  [fetch_adapters(): lax.ppermute(compact, 'grp', [(dev, dev ^ hop) for dev in range(32)])]
    psum x1 -> x0, waiting for transfers between devices: 129 us -> none  [fetch_adapters(): compact = lax.psum(compact, 'grp')]
    ppermute x0 -> x5, starting transfers between devices: none -> 13.5 us  [fetch_adapters(): lax.ppermute(compact, 'grp', [(dev, dev ^ hop) for dev in range(32)])]
    add x0 -> x5, other arithmetic: none -> 3.61 us  [fetch_adapters(): compact + lax.ppermute(compact, 'grp', [(dev, dev ^ hop) for dev in range...]
    unnamed x34 -> x36, local copies, waits for them, and re-layouts: 15.3 us -> 13.4 us
    unnamed x3 -> x2, waiting for transfers between devices: 36.7 us -> 34.9 us
  transfers between devices with their start and end apart: 7 -> 11, of which waited for: 5 -> 9; matrix products, arithmetic and copies ran while one was open for 16% -> 15% of each run, Pallas kernels for 0% -> 0%
where the time goes in v1:
time: 334 us; the launch traced here: 333 us
  waiting for transfers between devices  192 us (57%)
  local copies, waits for them, and re-layouts  37.5 us (11%)
  matrix products  34.4 us (10%)
  other arithmetic  29.9 us (9%)
  starting transfers between devices  23.8 us (7%)
  between operations  15.9 us (5%)
    ppermute x5, waiting for transfers between devices, fetch_adapters(): lax.ppermute(compact, 'grp', [(dev, dev ^ hop) for dev in range(32)])  138 us
    unnamed x2, waiting for transfers between devices  34.9 us
    ppermute x5, starting transfers between devices, fetch_adapters(): lax.ppermute(compact, 'grp', [(dev, dev ^ hop) for dev in range(32)])  13.5 us
    unnamed x36, local copies, waits for them, and re-layouts  13.4 us
    ppermute x2, waiting for transfers between devices, shifted(): return lax.ppermute(block, axis, route)  12.3 us
    sub x1, matrix products, local(): weights = jnp.exp(scores - row_top)  10.8 us
    dot_general x1, matrix products, local(): jnp.einsum('hts,shd->thd', weights_bf, value_all, preferred_element_type=...  8.93 us
  transfers between devices with their start and end apart: 11, of which 9 were waited for; matrix products, arithmetic and copies ran while one was open for 15% of the time, Pallas kernels for 0%

profile of v1, /device:TPU:4, one launch (start us, length us, event | category | flops | bytes accessed | tf_op | source)
XLA Modules:
  0.0 332.9 jit_solution(16684028391361807839)
XLA Ops:
  18.5 22.1 %collective-permute-done = bf16[16,32768]{1,0:T(8,128)(2,1)} collective-permute-done((bf16[16,32768]{1,0:T(8,128)(2,1)S(1)}, bf16[16,32768]{1,0:T(8,128)(2,1)}, u32[]{:S(2)}, u32[]{:S(2)}) %collective-permute-start) | collective-permute-done | bytes 1048608 | tf_op jit(solution)/shard_map/ppermute | solution.py:48
  43.7 23.9 %collective-permute-done.1 = bf16[16,32768]{1,0:T(8,128)(2,1)S(1)} collective-permute-done((bf16[16,32768]{1,0:T(8,128)(2,1)S(1)}, bf16[16,32768]{1,0:T(8,128)(2,1)S(1)}, u32[]{:S(2)}, u32[]{:S(2)}) %collective-permute-start.1) | collective-permute-done | bytes 1048608 | tf_op jit(solution)/shard_map/ppermute | solution.py:48
  69.9 3.1 fusion.2
  73.5 17.8 %collective-permute-done.2 = bf16[16,32768]{1,0:T(8,128)(2,1)S(1)} collective-permute-done((bf16[16,32768]{1,0:T(8,128)(2,1)S(1)}, bf16[16,32768]{1,0:T(8,128)(2,1)S(1)}, u32[]{:S(2)}, u32[]{:S(2)}) %collective-permute-start.2) | collective-permute-done | bytes 1048608 | tf_op jit(solution)/shard_map/ppermute | solution.py:48
  91.6 3.4 %collective-permute-start.3 = (bf16[16,32768]{1,0:T(8,128)(2,1)S(1)}, bf16[16,32768]{1,0:T(8,128)(2,1)}, u32[]{:S(2)}, u32[]{:S(2)}) collective-permute-start(bf16[16,32768]{1,0:T(8,128)(2,1)S(1)} %add.176), channel_id=1, source_target_pairs={{0,64},{8,72},{16,80},{24,88},{32,96},{40,104},{48,112},{56,120},{... | collective-permute-start | bytes 3145736 | tf_op jit(solution)/shard_map/ppermute | solution.py:48
  94.9 4.7 %copy.62 = bf16[2048,3,256]{0,2,1:T(8,128)(2,1)} copy(bf16[2048,3,256]{2,0,1:T(8,128)(2,1)} %param.14) | data formatting | bytes 6291456 | tf_op args[2]
  101.2 3.4 %fusion.4 = bf16[1024,2048]{1,0:T(8,128)(2,1)S(1)} fusion(bf16[1024,2048]{1,0:T(8,128)(2,1)} %param.12, f32[2048]{0:T(1024)S(1)} %copy-done.8, f32[1024]{0:T(1024)S(1)} %add_rsqrt_fusion), kind=kLoop, calls=%fused_computation.14 | loop fusion | flops 8388608 | bytes 8400896 | tf_op jit(solution)/shard_map/convert_element_type | solution.py:62
  104.5 33.7 %collective-permute-done.3 = bf16[16,32768]{1,0:T(8,128)(2,1)} collective-permute-done((bf16[16,32768]{1,0:T(8,128)(2,1)S(1)}, bf16[16,32768]{1,0:T(8,128)(2,1)}, u32[]{:S(2)}, u32[]{:S(2)}) %collective-permute-start.3) | collective-permute-done | bytes 1048608 | tf_op jit(solution)/shard_map/ppermute | solution.py:48
  139.7 6.5 %collective-permute-start.4 = (bf16[16,32768]{1,0:T(8,128)(2,1)S(1)}, bf16[16,32768]{1,0:T(8,128)(2,1)S(1)}, u32[]{:S(2)}, u32[]{:S(2)}) collective-permute-start(bf16[16,32768]{1,0:T(8,128)(2,1)S(1)} %add.177), channel_id=1, source_target_pairs={{0,128},{8,136},{16,144},{24,152},{32,160},{40,168},{48,176},{56,1... | collective-permute-start | bytes 3145736 | tf_op jit(solution)/shard_map/ppermute | solution.py:48
  146.2 5.1 %fusion.9 = f32[1024,3,256]{0,2,1:T(8,128)} fusion(bf16[1024,2048]{1,0:T(8,128)(2,1)S(1)} %fusion.4, bf16[2048,3,256]{0,2,1:T(8,128)(2,1)S(1)} %copy-done.4), kind=kOutput, calls=%fused_computation.21 | convolution fusion | flops 3221225472 | bytes 10485760 | tf_op jit(solution)/shard_map/dot_general | solution.py:133
  151.3 40.6 %collective-permute-done.4 = bf16[16,32768]{1,0:T(8,128)(2,1)S(1)} collective-permute-done((bf16[16,32768]{1,0:T(8,128)(2,1)S(1)}, bf16[16,32768]{1,0:T(8,128)(2,1)S(1)}, u32[]{:S(2)}, u32[]{:S(2)}) %collective-permute-start.4) | collective-permute-done | bytes 1048608 | tf_op jit(solution)/shard_map/ppermute | solution.py:48
  199.8 3.0 multiply_cosine_fusion
  202.8 2.7 collective-permute-done.6
  205.5 3.3 collective-permute-start.7
  210.0 3.5 %collective-permute-done.7 = f32[1024,48]{0,1:T(8,128)S(1)} collective-permute-done((f32[1024,48]{0,1:T(8,128)S(1)}, f32[1024,48]{0,1:T(8,128)S(1)}, u32[]{:S(2)}, u32[]{:S(2)}) %collective-permute-start.7) | collective-permute-done | bytes 196640 | tf_op jit(solution)/shard_map/ppermute | solution.py:27
  219.4 3.1 collective-permute-start.8
  230.4 2.6 subtract_convert_fusion
  233.1 12.3 %collective-permute-done.9 = bf16[1024,256]{0,1:T(8,128)(2,1)} collective-permute-done((bf16[1024,256]{0,1:T(8,128)(2,1)}, bf16[1024,256]{0,1:T(8,128)(2,1)}, u32[]{:S(2)}, u32[]{:S(2)}) %collective-permute-start.9) | collective-permute-done | bytes 524320 | tf_op jit(solution)/shard_map/ppermute | solution.py:16
  246.7 10.8 %fusion.49 = (f32[2,1024]{1,0:T(2,128)S(1)}, f32[2,1024,2048]{2,1,0:T(8,128)}) fusion(pred[1024,2048]{1,0:T(8,128)(4,1)} %pad_add_fusion, bf16[1024,2,128]{2,0,1:T(8,128)(2,1)S(1)} %maximum_convert_fusion, bf16[1024,2,128]{2,0,1:T(8,128)(2,1)S(1)} %copy.72, bf16[1024,2,64]{2,0,1:T(8,128)(2,1)} %get-tuple-element.7, bf16[1024,2,64]{2,0,1:T(8,128)(2,1)} %get-tuple-element.6), kind=kOutput, calls=%fused_computation.127 | convolution fusion | flops 1093666816 | bytes 20455424 | tf_op jit(solution)/shard_map/sub | solution.py:161
  257.5 8.9 %fusion.16 = bf16[2,128,1024]{2,1,0:T(8,128)(2,1)S(1)} fusion(f32[2,1024,2048]{2,1,0:T(8,128)} %get-tuple-element.23, f32[2,1024]{1,0:T(2,128)S(1)} %get-tuple-element.22, bf16[1024,2,128]{0,2,1:T(8,128)(2,1)S(1)} %slice_bitcast_fusion, bf16[1024,2,128]{0,2,1:T(8,128)(2,1)} %bitcast.22), kind=kOutput, calls=%fused_computation.32 | convolution fusion | flops 1084489728 | bytes 18358272 | tf_op jit(solution)/shard_map/hts,shd->thd/dot_general | solution.py:163
  266.7 3.2 convolution_convert_fusion
  269.9 6.4 %copy.82 = bf16[1024,2048]{0,1:T(8,128)(2,1)} copy(bf16[1024,2048]{1,0:T(8,128)(2,1)} %convolution_convert_fusion) | data formatting | bytes 8388608 | tf_op jit(solution)/shard_map/reshape | solution.py:173
  276.4 4.7 %pad_maximum_fusion = bf16[1024,8,272]{0,2,1:T(8,128)(2,1)} fusion(bf16[1024,8,16]{0,2,1:T(8,128)(2,1)S(1)} %broadcast_in_dim.158, bf16[1024,8,256]{0,2,1:T(8,128)(2,1)} %bitcast.97), kind=kLoop, calls=%fused_computation.20 | loop fusion | flops 8912896 | bytes 8912896 | tf_op jit(solution)/shard_map/concatenate | solution.py:171
  286.9 34.9 %reduce-scatter.4.cloned.1.call-done = bf16[272,1024]{1,0:T(8,128)(2,1)} async-done(((bf16[2176,1024]{1,0:T(8,128)(2,1)}), bf16[272,1024]{1,0:T(8,128)(2,1)}) %reduce-scatter.4.cloned.1.call-update) | async-done | bytes 557072
  (128 shorter events, 53.3 us)
Async XLA Ops:
  7.2 259.5 %copy-start = (bf16[256,2048]{1,0:T(8,128)(2,1)S(1)}, bf16[256,2048]{1,0:T(8,128)(2,1)}, u32[]{:S(2)}) copy-start(bf16[256,2048]{1,0:T(8,128)(2,1)} %param.15) | copy-start | bytes 3145732
  7.2 314.6 %reduce-scatter.4.cloned.1.call-start = ((), (), s32[]{:S(2)}) async-start(), calls=%async_computation.1 | async-start | bytes 5013504
  14.0 2.7 copy-start.9
  14.0 2.7 copy-start.10
  15.4 25.1 %collective-permute-start = (bf16[16,32768]{1,0:T(8,128)(2,1)S(1)}, bf16[16,32768]{1,0:T(8,128)(2,1)}, u32[]{:S(2)}, u32[]{:S(2)}) collective-permute-start(bf16[16,32768]{1,0:T(8,128)(2,1)S(1)} %select_select_fusion), channel_id=1, source_target_pairs={{0,8},{8,0},{16,24},{24,16},{32,40},{40,32},{48,56},{56,48},{64,72... | collective-permute-start | bytes 3145736 | tf_op jit(solution)/shard_map/ppermute | solution.py:48
  42.0 25.6 %collective-permute-start.1 = (bf16[16,32768]{1,0:T(8,128)(2,1)S(1)}, bf16[16,32768]{1,0:T(8,128)(2,1)S(1)}, u32[]{:S(2)}, u32[]{:S(2)}) collective-permute-start(bf16[16,32768]{1,0:T(8,128)(2,1)S(1)} %fusion.59), channel_id=1, source_target_pairs={{0,16},{8,24},{16,0},{24,8},{32,48},{40,56},{48,32},{56,40},{64,80... | collective-permute-start | bytes 3145736 | tf_op jit(solution)/shard_map/ppermute | solution.py:48
  67.8 23.5 %collective-permute-start.2 = (bf16[16,32768]{1,0:T(8,128)(2,1)S(1)}, bf16[16,32768]{1,0:T(8,128)(2,1)S(1)}, u32[]{:S(2)}, u32[]{:S(2)}) collective-permute-start(bf16[16,32768]{1,0:T(8,128)(2,1)S(1)} %add.175), channel_id=1, source_target_pairs={{0,32},{8,40},{16,48},{24,56},{32,0},{40,8},{48,16},{56,24},{64,96... | collective-permute-start | bytes 3145736 | tf_op jit(solution)/shard_map/ppermute | solution.py:48
  91.5 9.6 %copy-start.8 = (f32[2048]{0:T(1024)S(1)}, f32[2048]{0:T(1024)}, u32[]{:S(2)}) copy-start(f32[2048]{0:T(1024)} %param.13) | copy-start | bytes 24580
  91.6 46.7 %collective-permute-start.3 = (bf16[16,32768]{1,0:T(8,128)(2,1)S(1)}, bf16[16,32768]{1,0:T(8,128)(2,1)}, u32[]{:S(2)}, u32[]{:S(2)}) collective-permute-start(bf16[16,32768]{1,0:T(8,128)(2,1)S(1)} %add.176), channel_id=1, source_target_pairs={{0,64},{8,72},{16,80},{24,88},{32,96},{40,104},{48,112},{56,120},{... | collective-permute-start | bytes 3145736 | tf_op jit(solution)/shard_map/ppermute | solution.py:48
  101.2 45.0 %copy-start.4 = (bf16[2048,3,256]{0,2,1:T(8,128)(2,1)S(1)}, bf16[2048,3,256]{0,2,1:T(8,128)(2,1)}, u32[]{:S(2)}) copy-start(bf16[2048,3,256]{0,2,1:T(8,128)(2,1)} %copy.62) | copy-start | bytes 9437188
  104.5 46.8 %copy-start.2 = (bf16[1024,2048]{1,0:T(8,128)(2,1)}, bf16[1024,2048]{1,0:T(8,128)(2,1)S(1)}, u32[]{:S(2)}) copy-start(bf16[1024,2048]{1,0:T(8,128)(2,1)S(1)} %fusion.4) | copy-start | bytes 12582916
  139.7 52.2 %collective-permute-start.4 = (bf16[16,32768]{1,0:T(8,128)(2,1)S(1)}, bf16[16,32768]{1,0:T(8,128)(2,1)S(1)}, u32[]{:S(2)}, u32[]{:S(2)}) collective-permute-start(bf16[16,32768]{1,0:T(8,128)(2,1)S(1)} %add.177), channel_id=1, source_target_pairs={{0,128},{8,136},{16,144},{24,152},{32,160},{40,168},{48,176},{56,1... | collective-permute-start | bytes 3145736 | tf_op jit(solution)/shard_map/ppermute | solution.py:48
  193.0 3.6 %copy-start.3 = (pred[1024,1024]{1,0:T(8,128)(4,1)S(1)}, pred[1024,1024]{1,0:T(8,128)(4,1)}, u32[]{:S(2)}) copy-start(pred[1024,1024]{1,0:T(8,128)(4,1)} %fusion.11) | copy-start | bytes 3145732
  193.2 0.7 copy-start.6
  194.9 14.6 %copy-start.7 = (bf16[4,12288]{1,0:T(4,128)(2,1)S(1)}, bf16[4,12288]{1,0:T(4,128)(2,1)}, u32[]{:S(2)}) copy-start(bf16[4,12288]{1,0:T(4,128)(2,1)} %get-tuple-element.13) | copy-start | bytes 294916
  196.4 1.7 collective-permute-start.5
  198.1 7.4 %collective-permute-start.6 = (f32[1024,48]{0,1:T(8,128)S(1)}, f32[1024,48]{0,1:T(8,128)S(1)}, u32[]{:S(2)}, u32[]{:S(2)}) collective-permute-start(f32[1024,48]{0,1:T(8,128)S(1)} %add.180), channel_id=1, source_target_pairs={{0,2},{1,3},{2,0},{3,1},{4,6},{5,7},{6,4},{7,5},{8,10},{9,11},{10,... | collective-permute-start | bytes 589832 | tf_op jit(solution)/shard_map/ppermute | solution.py:27
  205.5 8.0 %collective-permute-start.7 = (f32[1024,48]{0,1:T(8,128)S(1)}, f32[1024,48]{0,1:T(8,128)S(1)}, u32[]{:S(2)}, u32[]{:S(2)}) collective-permute-start(f32[1024,48]{0,1:T(8,128)S(1)} %add.181), channel_id=1, source_target_pairs={{0,4},{1,5},{2,6},{3,7},{4,0},{5,1},{6,2},{7,3},{8,12},{9,13},{10,... | collective-permute-start | bytes 589832 | tf_op jit(solution)/shard_map/ppermute | solution.py:27
  216.0 1.8 copy-start.1
  219.4 38.1 %collective-permute-start.8 = (bf16[1024,256]{0,1:T(8,128)(2,1)}, bf16[1024,256]{0,1:T(8,128)(2,1)}, u32[]{:S(2)}, u32[]{:S(2)}) collective-permute-start(bf16[1024,256]{0,1:T(8,128)(2,1)} %bitcast.106), channel_id=1, source_target_pairs={{0,8},{8,16},{16,24},{24,32},{32,40},{40,48},{48,56},{56,64},{64,7... | collective-permute-start | bytes 1572872 | tf_op jit(solution)/shard_map/ppermute | solution.py:16
  227.0 18.4 %collective-permute-start.9 = (bf16[1024,256]{0,1:T(8,128)(2,1)}, bf16[1024,256]{0,1:T(8,128)(2,1)}, u32[]{:S(2)}, u32[]{:S(2)}) collective-permute-start(bf16[1024,256]{0,1:T(8,128)(2,1)} %bitcast.29), channel_id=1, source_target_pairs={{0,8},{8,16},{16,24},{24,32},{32,40},{40,48},{48,56},{56,64},{64,7... | collective-permute-start | bytes 1572872 | tf_op jit(solution)/shard_map/ppermute | solution.py:16
  281.1 0.7 copy-start.11
  281.1 1.3 copy-start.5
Sparse Core Ops, SparseCore 0:
  281.2 40.5 reduce-scatter.3
